TPU v7x, 256 devices: a whole 4x4x8 slice. The times are simulated.
256 devices in a mesh: dp: 8 (over z), expert: 32 (over y, x, core).
Axes of the slice: x: 4, y: 4, z: 8, core: 2. Of those that a mesh axis runs over, the one named last changes fastest.
Arguments:
- tokens: bfloat16 [32, 16, 7168], P('expert', 'dp'), may hold values from -6 to 6
- tangent: bfloat16 [32, 16, 7168], P('expert', 'dp'), may hold values from -52 to 52
- route_ids: int32 [32, 16, 8], P('expert', 'dp'), may hold values from 0 to 31, all different within a row; in each aligned block of 16 rows (0 to 15, 16 to 31, ..., all dimensions but the last counted through in order) at most 8 rows name the same one
- gate_fixed: int32 [32, 16, 8], P('expert', 'dp'), may hold values from 4096 to 65535
- gate_proj: bfloat16 [32, 7168, 2048], P('expert', None, 'dp'), may hold values from -0.0625 to 0.0625
- up_proj: bfloat16 [32, 7168, 2048], P('expert', None, 'dp'), may hold values from -0.0625 to 0.0625
- down_proj: bfloat16 [32, 2048, 7168], P('expert', 'dp'), may hold values from -0.125 to 0.125
Outputs:
- next_tangent: bfloat16 [32, 16, 7168], P('expert', 'dp')
- lipschitz: float32 [], replicated
Inputs may be any that keep to these rules, and one draw needn't show every extreme that they name: `route_ids`: each token names 8 different experts; within one group of 16 tokens no expert is named by more than 8 tokens.
All inputs are finite; a program needn't handle non-finite values.
Results may differ from a plain program's by a relative error of at most 0.0065.
Values may be sent and summed in bfloat16 or wider, within the bound.
No kernel may reach another device: no remote copies, remote signals or barrier semaphores. Data moves between devices by JAX's collectives and lax.ppermute only.
A program may use at most 128 MiB of HBM per device.

v0:
```python
import jax
import jax.numpy as jnp
from jax import lax
from jax.sharding import PartitionSpec as P


def silu_parts(gate_pre):
    sigmoid_val = jax.nn.sigmoid(gate_pre)
    return (gate_pre * sigmoid_val, sigmoid_val * (1.0 + gate_pre * (1.0 - sigmoid_val)))


def contract_last(left, right):
    return lax.dot_general(
        left, right, (((1,), (1,)), ((), ())), preferred_element_type=jnp.float32
    )


def send_back(partial_value):
    return lax.all_to_all(partial_value, "expert", split_axis=0, concat_axis=0, tiled=True)


def body(tokens, tangent, route_ids, gate_fixed, gate_proj, up_proj, down_proj):
    model_width = tokens.shape[2]
    tok_dev = tokens.shape[1]
    experts = lax.axis_size("expert")
    col_tokens, col_tangent, col_ids, col_gates = (
        lax.all_gather(tokens[0], "dp", axis=0, tiled=True),
        lax.all_gather(tangent[0], "dp", axis=0, tiled=True),
        lax.all_gather(route_ids[0], "dp", axis=0, tiled=True),
        lax.all_gather(gate_fixed[0], "dp", axis=0, tiled=True),
    )
    col_count = col_tokens.shape[0]
    top_count = col_ids.shape[1]
    capacity = min(col_count, 2 * col_count * top_count // experts)
    slot_total = experts * capacity
    flat_ids = col_ids.reshape(-1)
    experts_all = jnp.arange(experts, dtype=jnp.int32)
    onehot = (flat_ids[:, None] == experts_all[None, :]).astype(jnp.int32)
    earlier = jnp.cumsum(onehot, axis=0) - onehot
    slot_place = jnp.sum(earlier * onehot, axis=1)
    target = flat_ids * capacity + slot_place
    places = jnp.arange(slot_total, dtype=jnp.int32)
    matches = target[:, None] == places[None, :]
    route_map = (
        jnp.sum(matches.reshape(col_count, top_count, slot_total), axis=1).astype(jnp.bfloat16).T
    )
    gate_vals = col_gates.reshape(-1).astype(jnp.float32) / 65536.0
    combine_map = jnp.sum(
        jnp.where(matches, gate_vals[:, None], 0.0).reshape(col_count, top_count, slot_total),
        axis=1,
    )
    send_in = (
        jnp.dot(route_map, col_tokens, preferred_element_type=jnp.float32)
        .astype(jnp.bfloat16)
        .reshape(experts, capacity, model_width)
    )
    send_dir = (
        jnp.dot(route_map, col_tangent, preferred_element_type=jnp.float32)
        .astype(jnp.bfloat16)
        .reshape(experts, capacity, model_width)
    )
    weight_gate = gate_proj[0]
    weight_up = up_proj[0]
    weight_down = down_proj[0]
    hidden_dev = weight_gate.shape[1]
    rows_in = lax.all_to_all(send_in, "expert", split_axis=0, concat_axis=0, tiled=True)
    rows_dir = lax.all_to_all(send_dir, "expert", split_axis=0, concat_axis=0, tiled=True)
    groups_here = rows_in.shape[0]
    slots_here = rows_in.shape[1]
    flat_in = rows_in.reshape(-1, model_width)
    flat_dir = rows_dir.reshape(-1, model_width)
    gate_pre = jnp.dot(flat_in, weight_gate, preferred_element_type=jnp.float32)
    up_pre = jnp.dot(flat_in, weight_up, preferred_element_type=jnp.float32)
    gate_dir = jnp.dot(flat_dir, weight_gate, preferred_element_type=jnp.float32)
    up_dir = jnp.dot(flat_dir, weight_up, preferred_element_type=jnp.float32)
    silu_value, silu_slope = silu_parts(gate_pre)
    jvp_hidden = (silu_slope * gate_dir * up_pre + silu_value * up_dir).astype(jnp.bfloat16)
    partial_value = jnp.dot(jvp_hidden, weight_down, preferred_element_type=jnp.float32)
    returned = send_back(partial_value.reshape(groups_here, slots_here, model_width))
    gate_coef = (silu_slope * up_pre).reshape(groups_here, slots_here, hidden_dev)
    up_coef = silu_value.reshape(groups_here, slots_here, hidden_dev)
    returned, gate_coef, up_coef = (returned, gate_coef, up_coef)
    product_part = jnp.dot(
        combine_map,
        returned.reshape(slot_total, -1),
        precision=lax.Precision.HIGHEST,
        preferred_element_type=jnp.float32,
    )
    product_bf = lax.psum(product_part, "dp").astype(jnp.bfloat16)
    send_prod = (
        jnp.dot(route_map, product_bf, preferred_element_type=jnp.float32)
        .astype(jnp.bfloat16)
        .reshape(experts, capacity, model_width)
    )
    received = lax.all_to_all(send_prod, "expert", split_axis=0, concat_axis=0, tiled=True)
    grad_hidden = contract_last(received.reshape(slot_total, model_width), weight_down)
    grad_gate = (grad_hidden * gate_coef.reshape(slot_total, hidden_dev)).astype(jnp.bfloat16)
    grad_up = (grad_hidden * up_coef.reshape(slot_total, hidden_dev)).astype(jnp.bfloat16)
    vjp_part = contract_last(grad_gate, weight_gate) + contract_last(grad_up, weight_up)
    returned_two = send_back(vjp_part.reshape(experts, capacity, model_width))
    result_part = jnp.dot(
        combine_map,
        returned_two.reshape(slot_total, -1),
        precision=lax.Precision.HIGHEST,
        preferred_element_type=jnp.float32,
    )
    result = lax.psum_scatter(result_part, "dp", scatter_dimension=0, tiled=True)
    probe_f = tangent[0].astype(jnp.float32)
    probe_result, result_sq, probe_sq = lax.psum(
        (jnp.sum(probe_f * result), jnp.sum(result * result), jnp.sum(probe_f * probe_f)),
        ("dp", "expert"),
    )
    total_cells = lax.axis_size("dp") * lax.axis_size("expert") * tok_dev * model_width
    next_tangent = (result * lax.rsqrt(result_sq / total_cells + 1e-06)).astype(jnp.bfloat16)
    lipschitz = jnp.sqrt(probe_result / probe_sq)
    return (next_tangent[None], lipschitz)


def solution(mesh):
    return jax.shard_map(
        body,
        mesh=mesh,
        in_specs=(
            P("expert", "dp", None),
            P("expert", "dp", None),
            P("expert", "dp", None),
            P("expert", "dp", None),
            P("expert", None, "dp"),
            P("expert", None, "dp"),
            P("expert", "dp", None),
        ),
        out_specs=(P("expert", "dp", None), P()),
        check_vma=False,
    )
```

profile of v0, /device:TPU:1, one launch (start us, length us, event | category | flops | bytes accessed | tf_op | source)
XLA Modules:
  0.0 622.9 jit_solution(1392663835908994589)
XLA Ops:
  7.2 16.7 %all-gather = s32[1,16,8]{2,0,1:T(1,128)S(1)} all-gather(s32[1,2,8]{2,0,1:T(1,128)} %bitcast.102), channel_id=2, replica_groups=mesh['dp'=8,'expert'=32] {'dp'}, dimensions={1}, use_global_device_ids=true | all-gather | bytes 576 | tf_op jit(solution)/shard_map/all_gather | solution.py:29
  23.9 0.1 copy.40
  23.9 0.5 broadcast.53
  24.4 0.7 reduce.3
  25.1 0.1 eq.30
  25.2 0.1 fusion.68
  25.3 0.2 reduce_window_sum.11
  25.5 0.2 select_reduce_fusion.1
  25.7 0.1 reduce_sum.57
  25.7 0.1 copy.41
  25.8 0.1 copy.42
  25.9 0.1 convert_reduce_fusion
  26.0 0.8 copy.46
  26.8 19.3 %all-gather.2 = bf16[1,16,7168]{2,0,1:T(2,128)(2,1)S(1)} all-gather(bf16[1,2,7168]{2,0,1:T(2,128)(2,1)S(1)} %copy.46), channel_id=4, replica_groups=mesh['dp'=8,'expert'=32] {'dp'}, dimensions={1}, use_global_device_ids=true | all-gather | bytes 258048 | tf_op jit(solution)/shard_map/all_gather | solution.py:27
  46.1 3.0 fusion.1
  49.1 17.6 %all-to-all-start = ((bf16[32,8,7168]{2,1,0:T(8,128)(2,1)}), bf16[32,8,7168]{2,1,0:T(8,128)(2,1)}, u32[]{:S(2)}, u32[]{:S(2)}) async-start(bf16[32,8,7168]{2,1,0:T(8,128)(2,1)} %fusion.1), calls=%async_computation | async-start | bytes 7340032 | tf_op jit(solution)/shard_map/all_to_all | solution.py:66
  66.9 21.6 %all-gather.3 = bf16[1,16,7168]{2,0,1:T(2,128)(2,1)S(1)} all-gather(bf16[1,2,7168]{2,0,1:T(2,128)(2,1)S(1)} %copy.47), channel_id=5, replica_groups=mesh['dp'=8,'expert'=32] {'dp'}, dimensions={1}, use_global_device_ids=true | all-gather | bytes 258048 | tf_op jit(solution)/shard_map/all_gather | solution.py:28
  88.4 3.0 fusion.2
  91.4 20.8 %all-to-all-done = bf16[32,8,7168]{2,1,0:T(8,128)(2,1)} async-done(((bf16[32,8,7168]{2,1,0:T(8,128)(2,1)}), bf16[32,8,7168]{2,1,0:T(8,128)(2,1)}, u32[]{:S(2)}, u32[]{:S(2)}) %all-to-all-start) | async-done | bytes 3670048 | tf_op jit(solution)/shard_map/all_to_all | solution.py:66
  112.2 7.2 %all-to-all-start.1 = ((bf16[32,8,7168]{2,1,0:T(8,128)(2,1)}), bf16[32,8,7168]{2,1,0:T(8,128)(2,1)}, u32[]{:S(2)}, u32[]{:S(2)}) async-start(bf16[32,8,7168]{2,1,0:T(8,128)(2,1)} %fusion.2), calls=%async_computation.1 | async-start | bytes 7340032 | tf_op jit(solution)/shard_map/all_to_all | solution.py:67
  119.5 4.4 fusion.24
  123.9 3.2 fusion.16
  127.1 37.5 %all-to-all-done.1 = bf16[32,8,7168]{2,1,0:T(8,128)(2,1)} async-done(((bf16[32,8,7168]{2,1,0:T(8,128)(2,1)}), bf16[32,8,7168]{2,1,0:T(8,128)(2,1)}, u32[]{:S(2)}, u32[]{:S(2)}) %all-to-all-start.1) | async-done | bytes 3670048 | tf_op jit(solution)/shard_map/all_to_all | solution.py:67
  164.6 4.3 fusion.43
  168.9 11.2 %fusion.10 = f32[32,8,7168]{2,1,0:T(8,128)} fusion(bf16[1,256,7168]{2,1,0:T(8,128)(2,1)} %param.13, f32[256,256]{1,0:T(8,128)S(1)} %fusion.43, f32[256,256]{1,0:T(8,128)S(1)} %fusion.16, bf16[1,7168,256]{2,1,0:T(8,128)(2,1)} %param.11, bf16[32,8,7168]{2,1,0:T(8,128)(2,1)} %all-to-all-done.1, f32[256,256]{1,0:T(8,128)S(1)} %fusion.24), kind=kOutput, calls=%fused_computation.14 | convolution fusion | flops 1879769088 | bytes 19136512 | tf_op jit(solution)/shard_map/dot_general | solution.py:78
  180.0 7.8 %all-to-all-start.2 = ((f32[32,8,7168]{2,1,0:T(8,128)}), f32[32,8,7168]{2,1,0:T(8,128)}, u32[]{:S(2)}, u32[]{:S(2)}) async-start(f32[32,8,7168]{2,1,0:T(8,128)} %fusion.10), calls=%async_computation.2 | async-start | bytes 14680064 | tf_op jit(solution)/shard_map/all_to_all | solution.py:19
  187.8 0.0 all-reduce.5.cloned.1.call-start
  187.9 11.6 %all-gather.1 = s32[1,16,8]{2,0,1:T(1,128)S(1)} all-gather(s32[1,2,8]{2,0,1:T(1,128)S(1)} %bitcast.103), channel_id=3, replica_groups=mesh['dp'=8,'expert'=32] {'dp'}, dimensions={1}, use_global_device_ids=true | all-gather | bytes 576 | tf_op jit(solution)/shard_map/all_gather | solution.py:30
  199.5 0.1 copy.44
  199.6 0.1 copy.45
  199.7 0.1 select_reduce_fusion
  199.8 75.2 %all-to-all-done.2 = f32[32,8,7168]{2,1,0:T(8,128)} async-done(((f32[32,8,7168]{2,1,0:T(8,128)}), f32[32,8,7168]{2,1,0:T(8,128)}, u32[]{:S(2)}, u32[]{:S(2)}) %all-to-all-start.2) | async-done | bytes 7340064 | tf_op jit(solution)/shard_map/all_to_all | solution.py:19
  275.0 5.7 fusion.6
  280.7 26.0 %all-reduce.6 = bf16[16,7168]{1,0:T(8,128)(2,1)S(1)} all-reduce(f32[16,7168]{1,0:T(8,128)S(1)} %fusion.6), channel_id=1, replica_groups=mesh['dp'=8,'expert'=32] {'dp'}, use_global_device_ids=true, to_apply=%region_4.5 | all-reduce | flops 114688 | bytes 688128 | tf_op jit(solution)/shard_map/psum | solution.py:89
  306.7 1.1 fusion.3
  307.8 60.0 %all_to_all.25 = bf16[32,8,7168]{2,1,0:T(8,128)(2,1)S(1)} all-to-all(bf16[32,8,7168]{2,1,0:T(8,128)(2,1)S(1)} %fusion.3), channel_id=1, replica_groups=mesh['dp'=8,'expert'=32] {'expert'}, dimensions={0} | all-to-all | bytes 7340032 | tf_op jit(solution)/shard_map/all_to_all | solution.py:95
  367.9 1.1 fusion.8
  369.0 0.9 copy-done
  369.9 1.2 fusion.21
  371.1 0.9 copy-done.3
  371.9 1.2 fusion
  373.1 88.2 %all_to_all.26 = f32[32,8,7168]{2,1,0:T(8,128)S(1)} all-to-all(f32[32,8,7168]{2,1,0:T(8,128)S(1)} %fusion), channel_id=1, replica_groups=mesh['dp'=8,'expert'=32] {'expert'}, dimensions={0} | all-to-all | bytes 14680064 | tf_op jit(solution)/shard_map/all_to_all | solution.py:19
  461.4 4.3 fusion.4
  465.7 0.6 dynamic-slice
  467.0 62.5 %all-reduce.5.cloned.1.call-done = f32[16,7168]{1,0:T(8,128)} async-done(((f32[16,7168]{1,0:T(8,128)}), f32[16,7168]{1,0:T(8,128)}) %all-reduce.5.cloned.1.call-update) | async-done | bytes 458768
  529.5 1.7 fusion.69
  531.2 80.1 %all-reduce.1 = (f32[]{:T(128)}, f32[]{:T(128)}, f32[]{:T(128)}) all-reduce(f32[]{:T(128)} %get-tuple-element.3, f32[]{:T(128)} %get-tuple-element.2, f32[]{:T(128)} %get-tuple-element.4), channel_id=1, replica_groups=mesh['dp'=8,'expert'=32] {'dp','expert'}, use_global_device_ids=true, to_apply=%region_7.8 | all-reduce | flops 3 | bytes 24 | tf_op jit(solution)/shard_map/psum | solution.py:109
  613.3 1.6 fusion.72
  (16 shorter events, 0.1 us)
Async XLA Ops:
  49.1 17.7 %copy-start.4 = (bf16[1,2,7168]{2,1,0:T(2,128)(2,1)S(1)}, bf16[1,2,7168]{2,1,0:T(2,128)(2,1)}, u32[]{:S(2)}) copy-start(bf16[1,2,7168]{2,1,0:T(2,128)(2,1)} %param.8) | copy-start | bytes 86020
  49.1 63.1 %all-to-all-start = ((bf16[32,8,7168]{2,1,0:T(8,128)(2,1)}), bf16[32,8,7168]{2,1,0:T(8,128)(2,1)}, u32[]{:S(2)}, u32[]{:S(2)}) async-start(bf16[32,8,7168]{2,1,0:T(8,128)(2,1)} %fusion.1), calls=%async_computation | async-start | bytes 7340032 | tf_op jit(solution)/shard_map/all_to_all | solution.py:66
  112.2 52.4 %all-to-all-start.1 = ((bf16[32,8,7168]{2,1,0:T(8,128)(2,1)}), bf16[32,8,7168]{2,1,0:T(8,128)(2,1)}, u32[]{:S(2)}, u32[]{:S(2)}) async-start(bf16[32,8,7168]{2,1,0:T(8,128)(2,1)} %fusion.2), calls=%async_computation.1 | async-start | bytes 7340032 | tf_op jit(solution)/shard_map/all_to_all | solution.py:67
  119.4 4.4 copy-start.2
  180.0 7.9 %copy-start.5 = (s32[1,2,8]{2,1,0:T(2,128)S(1)}, s32[1,2,8]{2,1,0:T(2,128)}, u32[]{:S(2)}) copy-start(s32[1,2,8]{2,1,0:T(2,128)} %param.10) | copy-start | bytes 196
  180.0 95.0 %all-to-all-start.2 = ((f32[32,8,7168]{2,1,0:T(8,128)}), f32[32,8,7168]{2,1,0:T(8,128)}, u32[]{:S(2)}, u32[]{:S(2)}) async-start(f32[32,8,7168]{2,1,0:T(8,128)} %fusion.10), calls=%async_computation.2 | async-start | bytes 14680064 | tf_op jit(solution)/shard_map/all_to_all | solution.py:19
  187.8 341.6 %all-reduce.5.cloned.1.call-start = ((), (), s32[]{:S(2)}) async-start(), calls=%async_computation.5 | async-start | bytes 917504
  307.8 60.0 %copy-start.1 = (bf16[1,256,7168]{2,1,0:T(8,128)(2,1)S(1)}, bf16[1,256,7168]{2,1,0:T(8,128)(2,1)}, u32[]{:S(2)}) copy-start(bf16[1,256,7168]{2,1,0:T(8,128)(2,1)} %param.13) | copy-start | bytes 11010052
  367.9 2.0 copy-start
  369.9 2.0 copy-start.3
  461.4 4.4 copy-start.6
Sparse Core Ops, SparseCore 0:
  465.8 63.5 all-reduce.4
where the time goes:
time: 624 us; the launch traced here: 623 us
  blocking collectives  323 us (52%)
  waiting for transfers between devices  196 us (31%)
  matrix products  43.7 us (7%)
  starting transfers between devices  32.7 us (5%)
  between operations  18.1 us (3%)
    all_to_all x1, blocking collectives, send_back(): lax.all_to_all(partial_value, 'expert', split_axis=0, concat_axis=0, tile...  88.2 us
    psum x1, blocking collectives, body(): lax.psum((jnp.sum(probe_f * result), jnp.sum(result * result), jnp.sum(pr...  80.1 us
    all_to_all x1, waiting for transfers between devices, send_back(): lax.all_to_all(partial_value, 'expert', split_axis=0, concat_axis=0, tile...  75.2 us
    unnamed x2, waiting for transfers between devices  62.5 us
    all_to_all x1, blocking collectives, body(): lax.all_to_all(send_prod, 'expert', split_axis=0, concat_axis=0, tiled=True)  60 us
    all_to_all x1, waiting for transfers between devices, body(): lax.all_to_all(send_dir, 'expert', split_axis=0, concat_axis=0, tiled=True)  37.5 us
    psum x1, blocking collectives, body(): product_bf = lax.psum(product_part, 'dp').astype(jnp.bfloat16)  26 us
    all_gather x1, blocking collectives, body(): lax.all_gather(tangent[0], 'dp', axis=0, tiled=True)  21.6 us
  transfers between devices with their start and end apart: 4, of which 4 were waited for; matrix products, arithmetic and copies ran while one was open for 2% of the time, Pallas kernels for 0%

commit v1 on v0

--- a/solution.py
+++ b/solution.py
@@ -86,7 +86,7 @@
         precision=lax.Precision.HIGHEST,
         preferred_element_type=jnp.float32,
     )
-    product_bf = lax.psum(product_part, "dp").astype(jnp.bfloat16)
+    product_bf = jnp.sum(lax.all_gather(product_part, "dp"), axis=0).astype(jnp.bfloat16)
     send_prod = (
         jnp.dot(route_map, product_bf, preferred_element_type=jnp.float32)
         .astype(jnp.bfloat16)

time: 624 us -> 643 us (1.030)
  waiting for transfers between devices: 196 us -> 244 us
  blocking collectives: 323 us -> 290 us
    all_gather x0 -> x1, waiting for transfers between devices: none -> 47.8 us  [body(): lax.all_gather(product_part, 'dp')]
    psum x1 -> x0, blocking collectives: 26 us -> none  [body(): product_bf = lax.psum(product_part, 'dp').astype(jnp.bfloat16)]
    all_to_all x1, blocking collectives: 60 us -> 52.9 us  [body(): lax.all_to_all(send_prod, 'expert', split_axis=0, concat_axis=0, tiled=True)]
    unnamed x2 -> x3, waiting for transfers between devices: 62.5 us -> 63.3 us
  transfers between devices with their start and end apart: 4 -> 5, of which waited for: 4 -> 5; matrix products, arithmetic and copies ran while one was open for 2% -> 2% of each run, Pallas kernels for 0% -> 0%
where the time goes in v1:
time: 643 us; the launch traced here: 642 us
  blocking collectives  290 us (45%)
  waiting for transfers between devices  244 us (38%)
  matrix products  45.4 us (7%)
  starting transfers between devices  32.7 us (5%)
  between operations  18.1 us (3%)
  other arithmetic  6.88 us (1%)
    all_to_all x1, blocking collectives, send_back(): lax.all_to_all(partial_value, 'expert', split_axis=0, concat_axis=0, tile...  88.1 us
    psum x1, blocking collectives, body(): lax.psum((jnp.sum(probe_f * result), jnp.sum(result * result), jnp.sum(pr...  80.1 us
    all_to_all x1, waiting for transfers between devices, send_back(): lax.all_to_all(partial_value, 'expert', split_axis=0, concat_axis=0, tile...  75.2 us
    unnamed x3, waiting for transfers between devices  63.3 us
    all_to_all x1, blocking collectives, body(): lax.all_to_all(send_prod, 'expert', split_axis=0, concat_axis=0, tiled=True)  52.9 us
    all_gather x1, waiting for transfers between devices, body(): lax.all_gather(product_part, 'dp')  47.8 us
    all_to_all x1, waiting for transfers between devices, body(): lax.all_to_all(send_dir, 'expert', split_axis=0, concat_axis=0, tiled=True)  37.5 us
    all_gather x1, blocking collectives, body(): lax.all_gather(tangent[0], 'dp', axis=0, tiled=True)  21.6 us
  transfers between devices with their start and end apart: 5, of which 5 were waited for; matrix products, arithmetic and copies ran while one was open for 2% of the time, Pallas kernels for 0%

profile of v1, /device:TPU:1, one launch (start us, length us, event | category | flops | bytes accessed | tf_op | source)
XLA Modules:
  0.0 642.1 jit_solution(5502922496966831543)
XLA Ops:
  7.2 16.7 %all-gather = s32[1,16,8]{2,0,1:T(1,128)S(1)} all-gather(s32[1,2,8]{2,0,1:T(1,128)} %bitcast.104), channel_id=2, replica_groups=mesh['dp'=8,'expert'=32] {'dp'}, dimensions={1}, use_global_device_ids=true | all-gather | bytes 576 | tf_op jit(solution)/shard_map/all_gather | solution.py:29
  23.9 0.1 copy.40
  23.9 0.5 broadcast.53
  24.4 0.7 reduce.3
  25.1 0.1 eq.30
  25.2 0.1 fusion.68
  25.3 0.2 reduce_window_sum.11
  25.5 0.2 select_reduce_fusion.1
  25.7 0.1 reduce_sum.66
  25.7 0.1 copy.41
  25.8 0.1 copy.42
  25.9 0.1 convert_reduce_fusion
  26.0 0.8 copy.46
  26.8 19.3 %all-gather.2 = bf16[1,16,7168]{2,0,1:T(2,128)(2,1)S(1)} all-gather(bf16[1,2,7168]{2,0,1:T(2,128)(2,1)S(1)} %copy.46), channel_id=4, replica_groups=mesh['dp'=8,'expert'=32] {'dp'}, dimensions={1}, use_global_device_ids=true | all-gather | bytes 258048 | tf_op jit(solution)/shard_map/all_gather | solution.py:27
  46.1 3.0 fusion.1
  49.1 17.6 %all-to-all-start = ((bf16[32,8,7168]{2,1,0:T(8,128)(2,1)}), bf16[32,8,7168]{2,1,0:T(8,128)(2,1)}, u32[]{:S(2)}, u32[]{:S(2)}) async-start(bf16[32,8,7168]{2,1,0:T(8,128)(2,1)} %fusion.1), calls=%async_computation | async-start | bytes 7340032 | tf_op jit(solution)/shard_map/all_to_all | solution.py:66
  66.8 21.6 %all-gather.3 = bf16[1,16,7168]{2,0,1:T(2,128)(2,1)S(1)} all-gather(bf16[1,2,7168]{2,0,1:T(2,128)(2,1)S(1)} %copy.47), channel_id=5, replica_groups=mesh['dp'=8,'expert'=32] {'dp'}, dimensions={1}, use_global_device_ids=true | all-gather | bytes 258048 | tf_op jit(solution)/shard_map/all_gather | solution.py:28
  88.4 3.0 fusion.2
  91.4 20.7 %all-to-all-done = bf16[32,8,7168]{2,1,0:T(8,128)(2,1)} async-done(((bf16[32,8,7168]{2,1,0:T(8,128)(2,1)}), bf16[32,8,7168]{2,1,0:T(8,128)(2,1)}, u32[]{:S(2)}, u32[]{:S(2)}) %all-to-all-start) | async-done | bytes 3670048 | tf_op jit(solution)/shard_map/all_to_all | solution.py:66
  112.1 7.2 %all-to-all-start.1 = ((bf16[32,8,7168]{2,1,0:T(8,128)(2,1)}), bf16[32,8,7168]{2,1,0:T(8,128)(2,1)}, u32[]{:S(2)}, u32[]{:S(2)}) async-start(bf16[32,8,7168]{2,1,0:T(8,128)(2,1)} %fusion.2), calls=%async_computation.1 | async-start | bytes 7340032 | tf_op jit(solution)/shard_map/all_to_all | solution.py:67
  119.4 4.4 fusion.24
  123.8 3.2 fusion.16
  127.0 37.5 %all-to-all-done.1 = bf16[32,8,7168]{2,1,0:T(8,128)(2,1)} async-done(((bf16[32,8,7168]{2,1,0:T(8,128)(2,1)}), bf16[32,8,7168]{2,1,0:T(8,128)(2,1)}, u32[]{:S(2)}, u32[]{:S(2)}) %all-to-all-start.1) | async-done | bytes 3670048 | tf_op jit(solution)/shard_map/all_to_all | solution.py:67
  164.5 4.3 fusion.43
  168.8 11.2 %fusion.10 = f32[32,8,7168]{2,1,0:T(8,128)} fusion(bf16[1,256,7168]{2,1,0:T(8,128)(2,1)} %param.13, f32[256,256]{1,0:T(8,128)S(1)} %fusion.43, f32[256,256]{1,0:T(8,128)S(1)} %fusion.16, bf16[1,7168,256]{2,1,0:T(8,128)(2,1)} %param.11, bf16[32,8,7168]{2,1,0:T(8,128)(2,1)} %all-to-all-done.1, f32[256,256]{1,0:T(8,128)S(1)} %fusion.24), kind=kOutput, calls=%fused_computation.14 | convolution fusion | flops 1879769088 | bytes 19136512 | tf_op jit(solution)/shard_map/dot_general | solution.py:78
  180.0 7.8 %all-to-all-start.2 = ((f32[32,8,7168]{2,1,0:T(8,128)}), f32[32,8,7168]{2,1,0:T(8,128)}, u32[]{:S(2)}, u32[]{:S(2)}) async-start(f32[32,8,7168]{2,1,0:T(8,128)} %fusion.10), calls=%async_computation.2 | async-start | bytes 14680064 | tf_op jit(solution)/shard_map/all_to_all | solution.py:19
  187.9 11.6 %all-gather.1 = s32[1,16,8]{2,0,1:T(1,128)S(1)} all-gather(s32[1,2,8]{2,0,1:T(1,128)S(1)} %bitcast.105), channel_id=3, replica_groups=mesh['dp'=8,'expert'=32] {'dp'}, dimensions={1}, use_global_device_ids=true | all-gather | bytes 576 | tf_op jit(solution)/shard_map/all_gather | solution.py:30
  199.5 0.1 copy.44
  199.6 0.1 copy.45
  199.6 0.1 select_reduce_fusion
  199.8 75.2 %all-to-all-done.2 = f32[32,8,7168]{2,1,0:T(8,128)} async-done(((f32[32,8,7168]{2,1,0:T(8,128)}), f32[32,8,7168]{2,1,0:T(8,128)}, u32[]{:S(2)}, u32[]{:S(2)}) %all-to-all-start.2) | async-done | bytes 7340064 | tf_op jit(solution)/shard_map/all_to_all | solution.py:19
  275.0 7.4 %fusion.6 = f32[16,7168]{1,0:T(8,128)} fusion(f32[16,256]{1,0:T(8,128)S(1)} %select_reduce_fusion, f32[32,8,7168]{2,1,0:T(8,128)} %all-to-all-done.2), kind=kOutput, calls=%fused_computation.10 | convolution fusion | flops 352321536 | bytes 7815168 | tf_op jit(solution)/shard_map/dot_general | solution.py:83
  282.4 47.8 %all-gather.7.cloned.1.call-done = f32[128,7168]{1,0:T(8,128)} async-done(((f32[16,7168]{1,0:T(8,128)}), f32[128,7168]{1,0:T(8,128)}) %all-gather.7.cloned.1.call-update) | async-done | bytes 3670032 | tf_op jit(solution)/shard_map/all_gather | solution.py:89
  330.2 2.2 reduce_sum.69
  332.4 1.1 fusion.3
  333.6 52.9 %all_to_all.25 = bf16[32,8,7168]{2,1,0:T(8,128)(2,1)S(1)} all-to-all(bf16[32,8,7168]{2,1,0:T(8,128)(2,1)S(1)} %fusion.3), channel_id=1, replica_groups=mesh['dp'=8,'expert'=32] {'expert'}, dimensions={0} | all-to-all | bytes 7340032 | tf_op jit(solution)/shard_map/all_to_all | solution.py:95
  386.5 1.1 fusion.8
  387.6 0.9 copy-done
  388.5 1.2 fusion.21
  389.7 0.9 copy-done.3
  390.5 1.2 fusion
  391.7 88.1 %all_to_all.26 = f32[32,8,7168]{2,1,0:T(8,128)S(1)} all-to-all(f32[32,8,7168]{2,1,0:T(8,128)S(1)} %fusion), channel_id=1, replica_groups=mesh['dp'=8,'expert'=32] {'expert'}, dimensions={0} | all-to-all | bytes 14680064 | tf_op jit(solution)/shard_map/all_to_all | solution.py:19
  479.8 4.3 fusion.4
  484.2 0.6 dynamic-slice
  485.4 63.2 %all-reduce.4.cloned.1.call-done = f32[16,7168]{1,0:T(8,128)} async-done(((f32[16,7168]{1,0:T(8,128)}), f32[16,7168]{1,0:T(8,128)}) %all-reduce.4.cloned.1.call-update) | async-done | bytes 458768
  548.6 1.7 fusion.69
  550.3 80.1 %all-reduce.1 = (f32[]{:T(128)}, f32[]{:T(128)}, f32[]{:T(128)}) all-reduce(f32[]{:T(128)} %get-tuple-element.3, f32[]{:T(128)} %get-tuple-element.2, f32[]{:T(128)} %get-tuple-element.4), channel_id=1, replica_groups=mesh['dp'=8,'expert'=32] {'dp','expert'}, use_global_device_ids=true, to_apply=%region_7.8 | all-reduce | flops 3 | bytes 24 | tf_op jit(solution)/shard_map/psum | solution.py:109
  632.5 1.6 fusion.72
  (19 shorter events, 0.2 us)
Async XLA Ops:
  49.1 17.7 %copy-start.4 = (bf16[1,2,7168]{2,1,0:T(2,128)(2,1)S(1)}, bf16[1,2,7168]{2,1,0:T(2,128)(2,1)}, u32[]{:S(2)}) copy-start(bf16[1,2,7168]{2,1,0:T(2,128)(2,1)} %param.8) | copy-start | bytes 86020
  49.1 63.1 %all-to-all-start = ((bf16[32,8,7168]{2,1,0:T(8,128)(2,1)}), bf16[32,8,7168]{2,1,0:T(8,128)(2,1)}, u32[]{:S(2)}, u32[]{:S(2)}) async-start(bf16[32,8,7168]{2,1,0:T(8,128)(2,1)} %fusion.1), calls=%async_computation | async-start | bytes 7340032 | tf_op jit(solution)/shard_map/all_to_all | solution.py:66
  112.1 52.4 %all-to-all-start.1 = ((bf16[32,8,7168]{2,1,0:T(8,128)(2,1)}), bf16[32,8,7168]{2,1,0:T(8,128)(2,1)}, u32[]{:S(2)}, u32[]{:S(2)}) async-start(bf16[32,8,7168]{2,1,0:T(8,128)(2,1)} %fusion.2), calls=%async_computation.1 | async-start | bytes 7340032 | tf_op jit(solution)/shard_map/all_to_all | solution.py:67
  119.4 4.4 copy-start.2
  180.0 7.9 %copy-start.5 = (s32[1,2,8]{2,1,0:T(2,128)S(1)}, s32[1,2,8]{2,1,0:T(2,128)}, u32[]{:S(2)}) copy-start(s32[1,2,8]{2,1,0:T(2,128)} %param.10) | copy-start | bytes 196
  180.0 95.0 %all-to-all-start.2 = ((f32[32,8,7168]{2,1,0:T(8,128)}), f32[32,8,7168]{2,1,0:T(8,128)}, u32[]{:S(2)}, u32[]{:S(2)}) async-start(f32[32,8,7168]{2,1,0:T(8,128)} %fusion.10), calls=%async_computation.2 | async-start | bytes 14680064 | tf_op jit(solution)/shard_map/all_to_all | solution.py:19
  187.8 142.4 %all-gather.7.cloned.1.call-start = ((), (), s32[]{:S(2)}) async-start(), calls=%async_computation.5 | async-start | bytes 4128768 | tf_op jit(solution)/shard_map/all_gather | solution.py:89
  282.4 266.2 %all-reduce.4.cloned.1.call-start = ((), (), s32[]{:S(2)}) async-start(), calls=%async_computation.6 | async-start | bytes 917504
  333.6 52.9 %copy-start.1 = (bf16[1,256,7168]{2,1,0:T(8,128)(2,1)S(1)}, bf16[1,256,7168]{2,1,0:T(8,128)(2,1)}, u32[]{:S(2)}) copy-start(bf16[1,256,7168]{2,1,0:T(8,128)(2,1)} %param.13) | copy-start | bytes 11010052
  386.5 2.0 copy-start
  388.5 2.0 copy-start.3
  479.8 4.4 copy-start.6
Sparse Core Ops, SparseCore 0:
  282.5 47.6 all-gather.6
  484.3 64.3 all-reduce.3
